TPU v7x, 32 devices: a whole 2x2x4 slice. The times are simulated.
32 devices in a mesh: groups: 2 (over y), expert: 4 (over z), dp: 4 (over x, core).
Axes of the slice: x: 2, y: 2, z: 4, core: 2. Of those that a mesh axis runs over, the one named last changes fastest.
Arguments:
- out_grad: bfloat16 [4096, 2048], P(('groups', 'expert', 'dp')), parts along dimension 0, may hold values from -0.5 to 0.5
- gate_weights: bfloat16 [4096, 8], P(('groups', 'expert', 'dp')), parts along dimension 0, may hold values from 0.049804688 to 0.5
- expert_ids: int32 [4096, 8], P(('groups', 'expert', 'dp')), parts along dimension 0, may hold values from 0 to 31, all different within a row; in each aligned block of 128 rows (0 to 127, 128 to 255, ...) at most 36 rows name the same one
- hidden: bfloat16 [32, 8, 4, 36, 768], P('expert', ('groups', 'dp')), parts along dimension 1, may hold values from -6 to 6
- down_weight: bfloat16 [32, 768, 2048], P('expert', None, 'dp'), may hold values from -0.21875 to 0.21875
Outputs:
- weight_grad: float32 [64, 768, 2048], P(('groups', 'expert'), None, 'dp'), parts along dimension 0
- gate_grad: float32 [4096, 8], P(('groups', 'expert', 'dp')), parts along dimension 0
There are 2 independent parts, one for each index of `groups`. A program takes and returns all parts, laid end to end along the dimension named above; an argument that names none is the same for every part. Nothing has to cross between parts.
Inputs may be any that keep to these rules, and one draw needn't show every extreme that they name: `expert_ids`: each token names 8 different experts; within each block of 128 tokens (one device's tokens) no expert is named by more than 36 tokens, a bound that some block reaches.
All inputs are finite; a program needn't handle non-finite values.
Results may differ from a plain program's by a relative error of at most 0.0095.
Values may be sent and summed in bfloat16 or wider, within the bound.
No kernel may reach another device: no remote copies, remote signals or barrier semaphores. Data moves between devices by JAX's collectives and lax.ppermute only.
A program may use at most 128 MiB of HBM per device.

v0:
```python
import jax
import jax.numpy as jnp
from jax import lax
from jax.sharding import PartitionSpec as P


def per_device(out_grad, gate_weights, expert_ids, hidden, down_weight):
    tok_rows, top_count = expert_ids.shape
    row_width = out_grad.shape[1]
    local_count = hidden.shape[0]
    capacity = hidden.shape[3]
    peer_count = lax.axis_size("expert")
    shards = lax.axis_size("dp")
    expert_count = local_count * peer_count
    col_width = row_width // shards
    block_count = peer_count * shards
    f32 = jnp.float32
    bf16 = jnp.bfloat16
    my_dp = lax.axis_index("dp")
    fetched = lax.ppermute(hidden, "dp", [(j, j ^ 2) for j in range(shards)])
    paired = lax.ppermute(
        jnp.concatenate([hidden, fetched], axis=1), "dp", [(j, j ^ 1) for j in range(shards)]
    )
    pieces = [hidden, fetched, paired[:, 0:1], paired[:, 1:2]]
    piece_replica = [my_dp, my_dp ^ 2, my_dp ^ 1, my_dp ^ 3]
    meta = jnp.concatenate([expert_ids.astype(bf16), gate_weights], axis=1).reshape(-1)
    meta_len = meta.shape[0]
    meta_rows = -(-meta_len // col_width)
    meta = jnp.pad(meta, (0, meta_rows * col_width - meta_len)).reshape(meta_rows, 1, col_width)
    cols = out_grad.reshape(tok_rows, shards, col_width)
    cols = jnp.concatenate([cols, jnp.broadcast_to(meta, (meta_rows, shards, col_width))], axis=0)
    cols = lax.all_to_all(cols, "dp", split_axis=1, concat_axis=0, tiled=True)
    cols = cols.reshape(shards, tok_rows + meta_rows, col_width)
    got = lax.all_gather(cols, "expert", axis=0, tiled=False)
    got = got.reshape(block_count, tok_rows + meta_rows, col_width)
    grad_all = got[:, :tok_rows]
    meta_all = got[:, tok_rows:].reshape(block_count, meta_rows * col_width)[:, :meta_len]
    meta_all = meta_all.reshape(block_count, tok_rows, 2 * top_count)
    ids_all = meta_all[:, :, :top_count].astype(jnp.int32)
    gate_all = meta_all[:, :, top_count:]
    my_experts = lax.axis_index("expert") * local_count + jnp.arange(local_count, dtype=jnp.int32)
    hit = ids_all[:, :, :, None] == my_experts[None, None, None, :]
    chose = jnp.any(hit, axis=2)
    gate_hit = jnp.sum(jnp.where(hit, gate_all.astype(f32)[:, :, :, None], 0.0), axis=2)
    before = (jnp.arange(tok_rows)[:, None] < jnp.arange(tok_rows)[None, :]).astype(bf16)
    rank = jnp.einsum("bul,ut->btl", chose.astype(bf16), before, preferred_element_type=f32).astype(
        jnp.int32
    )
    slot_ids = jnp.arange(capacity, dtype=jnp.int32)
    chose_t = chose.transpose(0, 2, 1)
    rank_t = rank.transpose(0, 2, 1)
    gate_t = gate_hit.transpose(0, 2, 1)
    select = chose_t[:, :, None, :] & (rank_t[:, :, None, :] == slot_ids[None, None, :, None])
    select_gate = jnp.where(select, gate_t[:, :, None, :], 0.0).astype(bf16)
    grad_rows = jnp.einsum(
        "blct,btd->blcd", select.astype(bf16), grad_all, preferred_element_type=f32
    ).astype(bf16)
    scaled = jnp.einsum("blct,btd->blcd", select_gate, grad_all, preferred_element_type=f32).astype(
        bf16
    )
    grad_rows = grad_rows.reshape(peer_count, shards, local_count, capacity, col_width)
    scaled = scaled.reshape(peer_count, shards, local_count, capacity, col_width)
    weight_grad = None
    slot_part = jnp.zeros((peer_count, shards, local_count, capacity), f32)
    for piece, replica in zip(pieces, piece_replica):
        piece = piece[:, 0]
        scaled_r = lax.dynamic_index_in_dim(scaled, replica, axis=1, keepdims=False)
        rows_r = lax.dynamic_index_in_dim(grad_rows, replica, axis=1, keepdims=False)
        part = (
            jnp.einsum("lscf,slcd->lfd", piece, scaled_r, preferred_element_type=f32)
            .astype(bf16)
            .astype(f32)
        )
        weight_grad = part if weight_grad is None else weight_grad + part
        expert_out = jnp.einsum("lscf,lfd->slcd", piece, down_weight, preferred_element_type=f32)
        slot_r = jnp.sum(rows_r.astype(f32) * expert_out, axis=3)
        slot_part = lax.dynamic_update_index_in_dim(slot_part, slot_r, replica, axis=1)
    send_back = slot_part.reshape(block_count, local_count, capacity)
    returned = lax.all_to_all(send_back, ("expert", "dp"), split_axis=0, concat_axis=0, tiled=True)
    returned = returned.reshape(peer_count, shards, local_count, capacity)
    slot_grad = jnp.sum(returned, axis=1).reshape(expert_count, capacity)
    own_hit = expert_ids[:, :, None] == jnp.arange(expert_count, dtype=jnp.int32)[None, None, :]
    own_chose = jnp.any(own_hit, axis=1)
    own_rank = jnp.einsum(
        "ue,ut->te", own_chose.astype(bf16), before, preferred_element_type=f32
    ).astype(jnp.int32)
    own_slot = jnp.sum(jnp.where(own_hit, own_rank[:, None, :], 0), axis=2)
    by_slot = jnp.sum(jnp.where(own_hit[:, :, :, None], slot_grad[None, None], 0.0), axis=2)
    gate_grad = jnp.sum(
        jnp.where(own_slot[:, :, None] == slot_ids[None, None, :], by_slot, 0.0), axis=2
    )
    return (weight_grad, gate_grad)


def solution(mesh):
    return jax.shard_map(
        per_device,
        mesh=mesh,
        in_specs=(
            P(("groups", "expert", "dp"), None),
            P(("groups", "expert", "dp"), None),
            P(("groups", "expert", "dp"), None),
            P("expert", ("groups", "dp"), None, None, None),
            P("expert", None, "dp"),
        ),
        out_specs=(P(("groups", "expert"), None, "dp"), P(("groups", "expert", "dp"), None)),
        check_vma=False,
    )
```

profile of v0, /device:TPU:0, one launch (start us, length us, event | category | flops | bytes accessed | tf_op | source)
XLA Modules:
  0.0 151.6 jit_solution(17778870522974405558)
XLA Ops:
  7.2 0.7 convert_element_type.81
  7.9 0.7 pad_maximum_fusion.2
  8.6 0.1 copy.187
  8.8 0.2 copy.188
  9.0 1.3 copy.186
  10.4 0.2 pad_maximum_fusion.1
  10.6 0.5 copy.189
  11.1 13.3 %all_to_all.20 = bf16[132,4,512]{2,0,1:T(8,128)(2,1)} all-to-all(bf16[132,4,512]{2,0,1:T(8,128)(2,1)S(1)} %copy.189), channel_id=1, replica_groups=mesh['groups'=2,'expert'=4,'dp'=4] {'dp'}, dimensions={1} | all-to-all | bytes 1081344 | tf_op jit(solution)/shard_map/all_to_all | solution.py:32
  24.4 2.0 %copy.196 = bf16[8,1,4,36,768]{4,0,3,2,1:T(8,128)(2,1)S(1)} copy(bf16[8,1,4,36,768]{4,2,3,1,0:T(4,128)(2,1)} %param.8) | data formatting | bytes 3538944 | tf_op args[3]
  26.4 0.4 collective-permute-start
  26.9 0.6 fusion.51
  27.5 0.1 convolution_convert_fusion.3
  27.7 39.3 %collective-permute-done = bf16[8,1,4,36,768]{4,0,3,2,1:T(8,128)(2,1)S(1)} collective-permute-done((bf16[8,1,4,36,768]{4,0,3,2,1:T(8,128)(2,1)S(1)}, bf16[8,1,4,36,768]{4,0,3,2,1:T(8,128)(2,1)S(1)}, u32[]{:S(2)}, u32[]{:S(2)}) %collective-permute-start) | collective-permute-done | bytes 1769504 | tf_op jit(solution)/shard_map/ppermute | solution.py:20
  67.0 2.3 %pad_maximum_fusion = bf16[8,2,4,36,768]{4,0,3,2,1:T(8,128)(2,1)} fusion(bf16[8,1,4,36,768]{4,0,3,2,1:T(8,128)(2,1)S(1)} %collective-permute-done, bf16[8,1,4,36,768]{4,0,3,2,1:T(8,128)(2,1)S(1)} %copy.196), kind=kLoop, calls=%fused_computation.15 | loop fusion | flops 1769472 | bytes 7077888 | tf_op jit(solution)/shard_map/concatenate | solution.py:22
  69.3 4.3 %all-gather.3.cloned.1.call-done = bf16[16,132,1,512]{3,1,2,0:T(8,128)(2,1)} async-done(((bf16[4,132,1,512]{3,1,2,0:T(8,128)(2,1)}), bf16[16,132,1,512]{3,1,2,0:T(8,128)(2,1)}) %all-gather.3.cloned.1.call-update) | async-done | bytes 2162704 | tf_op jit(solution)/shard_map/all_gather | solution.py:34
  73.7 0.9 slice.24
  74.6 0.4 reshape_reshape.3
  75.0 1.0 fusion.56
  76.0 1.2 copy.226
  77.2 0.2 copy.233
  77.4 0.1 compare_reduce_fusion
  77.6 0.1 fusion.50
  77.7 0.1 convolution_convert_fusion.2
  77.9 1.5 convolution_convert_fusion.1
  79.4 0.1 copy-done.2
  79.5 1.5 %convolution_convert_fusion = bf16[16,8,36,512]{3,2,1,0:T(8,128)(2,1)S(1)} fusion(bf16[16,132,512]{2,1,0:T(8,128)(2,1)S(1)} %bitcast.135, bf16[16,8,128]{2,1,0:T(8,128)(2,1)S(1)} %bitcast.142, s32[16,8,128]{2,1,0:T(8,128)S(1)} %convolution_convert_fusion.2, pred[16,8,128]{2,1,0:T(8,128)(4,1)S(1)} %bitcast.141), kind=kOutput, calls=%fused_computation.16 | convolution fusion | flops 608108544 | bytes 6930432 | tf_op jit(solution)/shard_map/blct,btd->blcd/dot_general | solution.py:58
  81.0 4.1 %constant_dynamic-slice_fusion = (bf16[4,1,8,36,512]{4,3,2,1,0:T(8,128)(2,1)}, bf16[4,1,8,36,512]{4,3,2,1,0:T(8,128)(2,1)}, bf16[4,1,8,36,512]{4,3,2,1,0:T(8,128...) fusion(bf16[4,4,8,36,512]{4,3,2,1,0:T(8,128)(2,1)S(1)} %bitcast, ...), kind=kLoop, calls=%fused_computation.78 | loop fusion | bytes 18874384 | tf_op jit(solution)/shard_map/jit(dynamic_index_in_dim)/dynamic_slice | solution.py:68
  85.1 5.0 %fusion.12 = f32[4,8,36]{2,0,1:T(4,128)S(1)} fusion(bf16[4,1,8,36,512]{4,3,2,1,0:T(8,128)(2,1)} %get-tuple-element.21, bf16[8,4,36,768]{3,1,2,0:T(4,128)(2,1)} %bitcast.138, bf16[8,768,512]{2,1,0:T(8,128)(2,1)} %param.9), kind=kOutput, calls=%fused_computation.25 | convolution fusion | flops 907737984 | bytes 9245184 | tf_op jit(solution)/shard_map/lscf,lfd->slcd/dot_general | solution.py:75
  90.2 0.6 broadcast_in_dim.109
  90.8 0.6 copy_dynamic-update-slice_fusion.3
  91.4 4.3 %fusion.11 = f32[4,8,36]{2,0,1:T(4,128)S(1)} fusion(bf16[4,1,8,36,512]{4,3,2,1,0:T(8,128)(2,1)S(1)} %copy-done.10, bf16[8,1,4,36,768]{4,0,3,2,1:T(8,128)(2,1)S(1)} %copy-done.4, bf16[8,768,512]{2,1,0:T(8,128)(2,1)} %param.9), kind=kOutput, calls=%fused_computation.23 | convolution fusion | flops 907737984 | bytes 9245184 | tf_op jit(solution)/shard_map/lscf,lfd->slcd/dot_general | solution.py:75
  95.7 0.6 copy_dynamic-update-slice_fusion.2
  96.4 4.6 %fusion.22 = bf16[8,512,768,1]{2,1,3,0:T(8,128)(2,1)} fusion(bf16[8,4,36,768]{3,1,2,0:T(4,128)(2,1)S(1)} %bitcast.139, bf16[4,1,8,36,512]{4,3,2,1,0:T(8,128)(2,1)S(1)} %copy-done.9), kind=kOutput, calls=%fused_computation.39 | convolution fusion | flops 905969664 | bytes 9240576 | tf_op jit(solution)/shard_map/lscf,slcd->lfd/dot_general | solution.py:70
  101.0 2.3 %fusion.55 = (bf16[8,1,4,36,768]{4,0,3,2,1:T(8,128)(2,1)S(1)}, bf16[8,1,4,36,768]{4,0,3,2,1:T(8,128)(2,1)S(1)}) fusion(bf16[8,2,4,36,768]{4,0,3,2,1:T(8,128)(2,1)} %collective-permute-done.1), kind=kLoop, calls=%fused_computation.88 | loop fusion | bytes 7077888 | tf_op jit(solution)/shard_map/slice | solution.py:24
  103.4 1.6 %fusion.9 = f32[4,8,36]{2,0,1:T(4,128)S(1)} fusion(bf16[4,1,8,36,512]{4,3,2,1,0:T(8,128)(2,1)S(1)} %copy-done.8, bf16[8,768,512]{2,1,0:T(8,128)(2,1)S(1)} %bitcast.149, bf16[8,1,4,36,768]{4,0,3,2,1:T(8,128)(2,1)S(1)} %get-tuple-element.26), kind=kOutput, calls=%fused_computation.19 | convolution fusion | flops 907737984 | bytes 9245184 | tf_op jit(solution)/shard_map/lscf,lfd->slcd/dot_general | solution.py:75
  105.0 1.8 %fusion.10 = f32[4,8,36]{2,0,1:T(4,128)S(1)} fusion(bf16[4,1,8,36,512]{4,3,2,1,0:T(8,128)(2,1)S(1)} %copy-done.7, bf16[8,768,512]{2,1,0:T(8,128)(2,1)S(1)} %bitcast.149, bf16[8,1,4,36,768]{4,0,3,2,1:T(8,128)(2,1)S(1)} %get-tuple-element.27), kind=kOutput, calls=%fused_computation.21 | convolution fusion | flops 907737984 | bytes 9245184 | tf_op jit(solution)/shard_map/lscf,lfd->slcd/dot_general | solution.py:75
  106.8 0.6 copy_dynamic-update-slice_fusion.1
  107.4 0.6 copy_dynamic-update-slice_fusion
  108.0 1.6 %reshape.70 = f32[16,1,288]{2,1,0:T(1,128)} reshape(f32[16,8,36]{2,1,0:T(8,128)} %bitcast.43) | data formatting | bytes 36864
  109.5 4.1 %all-to-all-start.1 = ((f32[16,1,288]{2,1,0:T(1,128)}), f32[16,1,288]{2,1,0:T(1,128)}, u32[]{:S(2)}, u32[]{:S(2)}) async-start(f32[16,1,288]{2,1,0:T(1,128)} %reshape.70), calls=%async_computation.1 | async-start | bytes 49152 | tf_op jit(solution)/shard_map/all_to_all | solution.py:79
  113.7 3.4 %fusion.17 = bf16[8,768,512,1]{1,2,3,0:T(8,128)(2,1)S(1)} fusion(bf16[8,1,4,36,768]{4,0,3,2,1:T(8,128)(2,1)S(1)} %get-tuple-element.27, bf16[4,1,8,36,512]{4,3,2,1,0:T(8,128)(2,1)} %get-tuple-element.33), kind=kOutput, calls=%fused_computation.34 | convolution fusion | flops 905969664 | bytes 9240576 | tf_op jit(solution)/shard_map/lscf,slcd->lfd/dot_general | solution.py:70
  117.1 1.9 %fusion.18 = bf16[8,768,512,1]{1,2,3,0:T(8,128)(2,1)S(1)} fusion(bf16[8,1,4,36,768]{4,0,3,2,1:T(8,128)(2,1)S(1)} %get-tuple-element.26, bf16[4,1,8,36,512]{4,3,2,1,0:T(8,128)(2,1)S(1)} %copy-done), kind=kOutput, calls=%fused_computation.35 | convolution fusion | flops 905969664 | bytes 9240576 | tf_op jit(solution)/shard_map/lscf,slcd->lfd/dot_general | solution.py:70
  119.0 9.5 %fusion = f32[8,768,512]{1,2,0:T(8,128)} fusion(bf16[8,512,768,1]{2,1,3,0:T(8,128)(2,1)} %fusion.22, bf16[8,768,512,1]{1,2,3,0:T(8,128)(2,1)S(1)} %fusion.17, bf16[8,768,512,1]{1,2,3,0:T(8,128)(2,1)S(1)} %fusion.18, bf16[8,1,4,36,768]{4,0,3,2,1:T(8,128)(2,1)S(1)} %copy-done.5, bf16[4,1,8,36,512]{4,3,2,1,0:T(8,128)(2,1)} %get-tuple-element.35), kind=kOutput, calls=%fused_computation.3 | convolution fusion | flops 931135488 | bytes 34406400 | tf_op jit(solution)/shard_map/lscf,slcd->lfd/dot_general | solution.py:70
  128.5 12.6 %copy.216 = f32[8,768,512]{2,1,0:T(8,128)} copy(f32[8,768,512]{1,2,0:T(8,128)} %fusion) | data formatting | bytes 25165824
  141.1 0.5 broadcast.17
  141.6 1.4 reduce
  143.3 0.8 select_reduce_fusion
  144.1 0.6 select_reduce_fusion.1
  (44 shorter events, 0.6 us)
Async XLA Ops:
  7.2 66.5 %all-gather.3.cloned.1.call-start = ((), (), s32[]{:S(2)}) async-start(), calls=%async_computation.2 | async-start | bytes 2785280 | tf_op jit(solution)/shard_map/all_gather | solution.py:34
  24.4 2.5 %copy-start.12 = (s32[128,8]{0,1:T(8,128)S(1)}, s32[128,8]{0,1:T(8,128)}, u32[]{:S(2)}) copy-start(s32[128,8]{0,1:T(8,128)} %param.7) | copy-start | bytes 12292
  26.4 40.5 %collective-permute-start = (bf16[8,1,4,36,768]{4,0,3,2,1:T(8,128)(2,1)S(1)}, bf16[8,1,4,36,768]{4,0,3,2,1:T(8,128)(2,1)S(1)}, u32[]{:S(2)}, u32[]{:S(2)}) collective-permute-start(bf16[8,1,4,36,768]{4,0,3,2,1:T(8,128)(2,1)S(1)} %copy.196), channel_id=1, source_target_pairs={{0,2},{1,3},{2,0},{3,1},{4,6},{5,7},{6,4},{7,5},{8,10},{9,11},{10,... | collective-permute-start | bytes 5308424 | tf_op jit(solution)/shard_map/ppermute | solution.py:20
  67.0 2.4 %copy-start.3 = (bf16[8,1,4,36,768]{4,0,3,2,1:T(8,128)(2,1)}, bf16[8,1,4,36,768]{4,0,3,2,1:T(8,128)(2,1)S(1)}, u32[]{:S(2)}) copy-start(bf16[8,1,4,36,768]{4,0,3,2,1:T(8,128)(2,1)S(1)} %collective-permute-done) | copy-start | bytes 5308420
  69.3 31.7 %collective-permute-start.1 = (bf16[8,2,4,36,768]{4,0,3,2,1:T(8,128)(2,1)}, bf16[8,2,4,36,768]{4,0,3,2,1:T(8,128)(2,1)}, u32[]{:S(2)}, u32[]{:S(2)}) collective-permute-start(bf16[8,2,4,36,768]{4,0,3,2,1:T(8,128)(2,1)} %pad_maximum_fusion), channel_id=1, source_target_pairs={{0,1},{1,0},{2,3},{3,2},{4,5},{5,4},{6,7},{7,6},{8,9},{9,8},{10,11... | collective-permute-start | bytes 10616840 | tf_op jit(solution)/shard_map/ppermute | solution.py:21
  75.0 2.9 %copy-start.1 = (bf16[16,132,1,512]{3,1,2,0:T(8,128)(2,1)S(1)}, bf16[16,132,1,512]{3,1,2,0:T(8,128)(2,1)}, u32[]{:S(2)}) copy-start(bf16[16,132,1,512]{3,1,2,0:T(8,128)(2,1)} %all-gather.3.cloned.1.call-done) | copy-start | bytes 6488068
  77.9 1.6 %copy-start.2 = (bf16[16,132,1,512]{3,1,2,0:T(8,128)(2,1)S(1)}, bf16[16,132,1,512]{3,1,2,0:T(8,128)(2,1)}, u32[]{:S(2)}) copy-start(bf16[16,132,1,512]{3,1,2,0:T(8,128)(2,1)} %all-gather.3.cloned.1.call-done) | copy-start | bytes 6488068
  85.1 6.3 %copy-start.4 = (bf16[8,1,4,36,768]{4,0,3,2,1:T(8,128)(2,1)S(1)}, bf16[8,1,4,36,768]{4,0,3,2,1:T(8,128)(2,1)}, u32[]{:S(2)}) copy-start(bf16[8,1,4,36,768]{4,0,3,2,1:T(8,128)(2,1)} %copy-done.3) | copy-start | bytes 5308420
  85.1 6.3 %copy-start.10 = (bf16[4,1,8,36,512]{4,3,2,1,0:T(8,128)(2,1)S(1)}, bf16[4,1,8,36,512]{4,3,2,1,0:T(8,128)(2,1)}, u32[]{:S(2)}) copy-start(bf16[4,1,8,36,512]{4,3,2,1,0:T(8,128)(2,1)} %get-tuple-element.20) | copy-start | bytes 3538948
  91.4 5.0 %copy-start.6 = (bf16[8,1,4,36,768]{4,2,3,1,0:T(4,128)(2,1)S(1)}, bf16[8,1,4,36,768]{4,2,3,1,0:T(4,128)(2,1)}, u32[]{:S(2)}) copy-start(bf16[8,1,4,36,768]{4,2,3,1,0:T(4,128)(2,1)} %param.8) | copy-start | bytes 5308420
  91.4 5.0 %copy-start.9 = (bf16[4,1,8,36,512]{4,3,2,1,0:T(8,128)(2,1)S(1)}, bf16[4,1,8,36,512]{4,3,2,1,0:T(8,128)(2,1)}, u32[]{:S(2)}) copy-start(bf16[4,1,8,36,512]{4,3,2,1,0:T(8,128)(2,1)} %get-tuple-element.32) | copy-start | bytes 3538948
  91.4 12.0 %slice-start = ((s8[6291456]{0:T(1024)(128)(4,1)}), s8[2097152]{0:T(1024)(128)(4,1)S(1)}, s32[]{:S(2)}) async-start(s8[6291456]{0:T(1024)(128)(4,1)} %bitcast.148), calls=%async_computation.3 | async-start | bytes 4194304
  96.4 7.0 %slice-start.1 = ((s8[6291456]{0:T(1024)(128)(4,1)}), s8[4194304]{0:T(1024)(128)(4,1)S(1)}, s32[]{:S(2)}) async-start(s8[6291456]{0:T(1024)(128)(4,1)} %bitcast.148), calls=%async_computation.4 | async-start | bytes 8388608
  101.0 2.4 %copy-start.8 = (bf16[4,1,8,36,512]{4,3,2,1,0:T(8,128)(2,1)S(1)}, bf16[4,1,8,36,512]{4,3,2,1,0:T(8,128)(2,1)}, u32[]{:S(2)}) copy-start(bf16[4,1,8,36,512]{4,3,2,1,0:T(8,128)(2,1)} %get-tuple-element.18) | copy-start | bytes 3538948
  103.4 1.6 %copy-start.7 = (bf16[4,1,8,36,512]{4,3,2,1,0:T(8,128)(2,1)S(1)}, bf16[4,1,8,36,512]{4,3,2,1,0:T(8,128)(2,1)}, u32[]{:S(2)}) copy-start(bf16[4,1,8,36,512]{4,3,2,1,0:T(8,128)(2,1)} %get-tuple-element.19) | copy-start | bytes 3538948
  109.5 31.6 %all-to-all-start.1 = ((f32[16,1,288]{2,1,0:T(1,128)}), f32[16,1,288]{2,1,0:T(1,128)}, u32[]{:S(2)}, u32[]{:S(2)}) async-start(f32[16,1,288]{2,1,0:T(1,128)} %reshape.70), calls=%async_computation.1 | async-start | bytes 49152 | tf_op jit(solution)/shard_map/all_to_all | solution.py:79
  113.7 3.4 %copy-start = (bf16[4,1,8,36,512]{4,3,2,1,0:T(8,128)(2,1)S(1)}, bf16[4,1,8,36,512]{4,3,2,1,0:T(8,128)(2,1)}, u32[]{:S(2)}) copy-start(bf16[4,1,8,36,512]{4,3,2,1,0:T(8,128)(2,1)} %get-tuple-element.34) | copy-start | bytes 3538948
  117.1 2.0 %copy-start.5 = (bf16[8,1,4,36,768]{4,0,3,2,1:T(8,128)(2,1)S(1)}, bf16[8,1,4,36,768]{4,0,3,2,1:T(8,128)(2,1)}, u32[]{:S(2)}) copy-start(bf16[8,1,4,36,768]{4,0,3,2,1:T(8,128)(2,1)} %copy-done.3) | copy-start | bytes 5308420
  128.5 14.8 %copy-start.11 = (pred[128,8,32]{0,2,1:T(8,128)(4,1)S(1)}, pred[128,8,32]{0,2,1:T(8,128)(4,1)}, u32[]{:S(2)}) copy-start(pred[128,8,32]{0,2,1:T(8,128)(4,1)} %get-tuple-element.31) | copy-start | bytes 98308
Sparse Core Ops, SparseCore 0:
  24.6 49.0 all-gather.2
where the time goes:
time: 152 us
  waiting for transfers between devices  43.6 us (29%)
  matrix products  35.5 us (23%)
  local copies, waits for them, and re-layouts  32.5 us (21%)
  between operations  14.3 us (9%)
  blocking collectives  13.3 us (9%)
  other arithmetic  7.75 us (5%)
  starting transfers between devices  4.59 us (3%)
    ppermute x1, waiting for transfers between devices, per_device(): fetched = lax.ppermute(hidden, 'dp', [(j, j ^ 2) for j in range(shards)])  39.3 us
    dot_general x4, matrix products, per_device(): jnp.einsum('lscf,slcd->lfd', piece, scaled_r, preferred_element_type=f32)  19.4 us
    unnamed x37, local copies, waits for them, and re-layouts  19.2 us
    all_to_all x1, blocking collectives, per_device(): cols = lax.all_to_all(cols, 'dp', split_axis=1, concat_axis=0, tiled=True)  13.3 us
    dot_general x4, matrix products, per_device(): jnp.einsum('lscf,lfd->slcd', piece, down_weight, preferred_element_type=f32)  12.7 us
    all_gather x1, waiting for transfers between devices, per_device(): got = lax.all_gather(cols, 'expert', axis=0, tiled=False)  4.34 us
    all_to_all x1, starting transfers between devices, per_device(): lax.all_to_all(send_back, ('expert', 'dp'), split_axis=0, concat_axis=0,...  4.13 us
    dynamic_slice x1, local copies, waits for them, and re-layouts, per_device(): lax.dynamic_index_in_dim(grad_rows, replica, axis=1, keepdims=False)  4.08 us
  transfers between devices with their start and end apart: 4, of which 2 were waited for; matrix products, arithmetic and copies ran while one was open for 39% of the time, Pallas kernels for 0%

commit v1 on v0

--- a/solution.py
+++ b/solution.py
@@ -2,6 +2,13 @@
 import jax.numpy as jnp
 from jax import lax
 from jax.sharding import PartitionSpec as P
+
+
+def plan_vector(inp):
+    side_arr = jnp.stack(jnp.split(inp, lax.axis_size("dp"), axis=1))
+    val2 = lax.all_to_all(side_arr, axis_name="dp", split_axis=0, concat_axis=0)
+    z_new = jnp.concatenate(val2, axis=0)
+    return z_new
 
 
 def per_device(out_grad, gate_weights, expert_ids, hidden, down_weight):
@@ -29,7 +36,7 @@
     meta = jnp.pad(meta, (0, meta_rows * col_width - meta_len)).reshape(meta_rows, 1, col_width)
     cols = out_grad.reshape(tok_rows, shards, col_width)
     cols = jnp.concatenate([cols, jnp.broadcast_to(meta, (meta_rows, shards, col_width))], axis=0)
-    cols = lax.all_to_all(cols, "dp", split_axis=1, concat_axis=0, tiled=True)
+    cols = plan_vector(cols)
     cols = cols.reshape(shards, tok_rows + meta_rows, col_width)
     got = lax.all_gather(cols, "expert", axis=0, tiled=False)
     got = got.reshape(block_count, tok_rows + meta_rows, col_width)

time: 152 us -> 153 us (level)
    unnamed x37 -> x39, local copies, waits for them, and re-layouts: 19.2 us -> 17.7 us
  transfers between devices with their start and end apart: 4 -> 4, of which waited for: 2 -> 2; matrix products, arithmetic and copies ran while one was open for 39% -> 38% of each run, Pallas kernels for 0% -> 0%
where the time goes in v1:
time: 153 us; the launch traced here: 152 us
  waiting for transfers between devices  45.1 us (29%)
  matrix products  35.4 us (23%)
  local copies, waits for them, and re-layouts  31 us (20%)
  between operations  14.3 us (9%)
  blocking collectives  13.4 us (9%)
  other arithmetic  7.99 us (5%)
  starting transfers between devices  4.59 us (3%)
    ppermute x1, waiting for transfers between devices, per_device(): fetched = lax.ppermute(hidden, 'dp', [(j, j ^ 2) for j in range(shards)])  39.3 us
    dot_general x4, matrix products, per_device(): jnp.einsum('lscf,slcd->lfd', piece, scaled_r, preferred_element_type=f32)  19.4 us
    unnamed x39, local copies, waits for them, and re-layouts  17.7 us
    all_to_all x1, blocking collectives, plan_vector(): val2 = lax.all_to_all(side_arr, axis_name='dp', split_axis=0, concat_axis=0)  13.4 us
    dot_general x4, matrix products, per_device(): jnp.einsum('lscf,lfd->slcd', piece, down_weight, preferred_element_type=f32)  12.7 us
    all_gather x1, waiting for transfers between devices, per_device(): got = lax.all_gather(cols, 'expert', axis=0, tiled=False)  5.8 us
    all_to_all x1, starting transfers between devices, per_device(): lax.all_to_all(send_back, ('expert', 'dp'), split_axis=0, concat_axis=0,...  4.13 us
    dynamic_slice x1, local copies, waits for them, and re-layouts, per_device(): lax.dynamic_index_in_dim(grad_rows, replica, axis=1, keepdims=False)  4.08 us
  transfers between devices with their start and end apart: 4, of which 2 were waited for; matrix products, arithmetic and copies ran while one was open for 38% of the time, Pallas kernels for 0%

profile of v1, /device:TPU:0, one launch (start us, length us, event | category | flops | bytes accessed | tf_op | source)
XLA Modules:
  0.0 151.9 jit_solution(13288997874657462983)
XLA Ops:
  7.2 0.7 convert_element_type.81
  7.9 0.7 pad_maximum_fusion.3
  8.6 0.1 copy.162
  8.8 0.2 copy.163
  9.0 1.3 copy.161
  10.4 0.2 fusion.55
  10.6 0.2 pad_maximum_fusion.1
  10.9 0.5 copy.164
  11.4 13.4 %all_to_all.10 = bf16[4,132,1,512]{3,1,2,0:T(8,128)(2,1)} all-to-all(bf16[4,132,1,512]{3,1,2,0:T(8,128)(2,1)S(1)} %copy.164), channel_id=1, replica_groups=mesh['groups'=2,'expert'=4,'dp'=4] {'dp'}, dimensions={0} | all-to-all | bytes 1081344 | tf_op jit(solution)/shard_map/all_to_all | solution.py:9
  24.8 0.5 copy.170
  25.4 0.4 collective-permute-start
  25.8 0.6 fusion.58
  26.4 0.1 convolution_convert_fusion.3
  26.6 39.3 %collective-permute-done = bf16[8,1,4,36,768]{4,0,3,2,1:T(8,128)(2,1)S(1)} collective-permute-done((bf16[8,1,4,36,768]{4,0,3,2,1:T(8,128)(2,1)S(1)}, bf16[8,1,4,36,768]{4,0,3,2,1:T(8,128)(2,1)S(1)}, u32[]{:S(2)}, u32[]{:S(2)}) %collective-permute-start) | collective-permute-done | bytes 1769504 | tf_op jit(solution)/shard_map/ppermute | solution.py:27
  65.9 2.3 %pad_maximum_fusion = bf16[8,2,4,36,768]{4,0,3,2,1:T(8,128)(2,1)} fusion(bf16[8,1,4,36,768]{4,0,3,2,1:T(8,128)(2,1)S(1)} %collective-permute-done, bf16[8,1,4,36,768]{4,0,3,2,1:T(8,128)(2,1)S(1)} %copy.170), kind=kLoop, calls=%fused_computation.15 | loop fusion | flops 1769472 | bytes 7077888 | tf_op jit(solution)/shard_map/concatenate | solution.py:29
  68.3 5.8 %all-gather.3.cloned.1.call-done = bf16[16,132,1,512]{3,1,2,0:T(8,128)(2,1)} async-done(((bf16[4,132,1,512]{3,1,2,0:T(8,128)(2,1)}), bf16[16,132,1,512]{3,1,2,0:T(8,128)(2,1)}) %all-gather.3.cloned.1.call-update) | async-done | bytes 2162704 | tf_op jit(solution)/shard_map/all_gather | solution.py:41
  74.1 0.9 slice.24
  75.0 0.4 reshape_reshape.3
  75.4 1.0 fusion.63
  76.4 1.2 copy.200
  77.6 0.2 copy.207
  77.8 0.1 compare_reduce_fusion
  78.0 0.1 fusion.50
  78.1 0.1 convolution_convert_fusion.2
  78.3 1.5 convolution_convert_fusion.1
  79.9 1.5 %convolution_convert_fusion = bf16[16,8,36,512]{3,2,1,0:T(8,128)(2,1)S(1)} fusion(bf16[16,132,512]{2,1,0:T(8,128)(2,1)S(1)} %bitcast.138, bf16[16,8,128]{2,1,0:T(8,128)(2,1)S(1)} %bitcast.144, s32[16,8,128]{2,1,0:T(8,128)S(1)} %convolution_convert_fusion.2, pred[16,8,128]{2,1,0:T(8,128)(4,1)S(1)} %bitcast.143), kind=kOutput, calls=%fused_computation.16 | convolution fusion | flops 608108544 | bytes 6930432 | tf_op jit(solution)/shard_map/blct,btd->blcd/dot_general | solution.py:65
  81.4 4.1 %constant_dynamic-slice_fusion = (bf16[4,1,8,36,512]{4,3,2,1,0:T(8,128)(2,1)}, bf16[4,1,8,36,512]{4,3,2,1,0:T(8,128)(2,1)}, bf16[4,1,8,36,512]{4,3,2,1,0:T(8,128...) fusion(bf16[4,4,8,36,512]{4,3,2,1,0:T(8,128)(2,1)S(1)} %bitcast, ...), kind=kLoop, calls=%fused_computation.92 | loop fusion | bytes 18874384 | tf_op jit(solution)/shard_map/jit(dynamic_index_in_dim)/dynamic_slice | solution.py:75
  85.5 5.0 %fusion.12 = f32[4,8,36]{2,0,1:T(4,128)S(1)} fusion(bf16[4,1,8,36,512]{4,3,2,1,0:T(8,128)(2,1)} %get-tuple-element.19, bf16[8,4,36,768]{3,1,2,0:T(4,128)(2,1)} %bitcast.140, bf16[8,768,512]{2,1,0:T(8,128)(2,1)} %param.9), kind=kOutput, calls=%fused_computation.25 | convolution fusion | flops 907737984 | bytes 9245184 | tf_op jit(solution)/shard_map/lscf,lfd->slcd/dot_general | solution.py:82
  90.5 0.6 broadcast_in_dim.109
  91.2 0.6 copy_dynamic-update-slice_fusion.3
  91.8 4.3 %fusion.11 = f32[4,8,36]{2,0,1:T(4,128)S(1)} fusion(bf16[4,1,8,36,512]{4,3,2,1,0:T(8,128)(2,1)S(1)} %copy-done.11, bf16[8,1,4,36,768]{4,0,3,2,1:T(8,128)(2,1)S(1)} %copy-done.4, bf16[8,768,512]{2,1,0:T(8,128)(2,1)} %param.9), kind=kOutput, calls=%fused_computation.23 | convolution fusion | flops 907737984 | bytes 9245184 | tf_op jit(solution)/shard_map/lscf,lfd->slcd/dot_general | solution.py:82
  96.1 0.6 copy_dynamic-update-slice_fusion.2
  96.8 4.6 %fusion.22 = bf16[8,512,768,1]{2,1,3,0:T(8,128)(2,1)} fusion(bf16[8,4,36,768]{3,1,2,0:T(4,128)(2,1)S(1)} %bitcast.141, bf16[4,1,8,36,512]{4,3,2,1,0:T(8,128)(2,1)S(1)} %copy-done.10), kind=kOutput, calls=%fused_computation.42 | convolution fusion | flops 905969664 | bytes 9240576 | tf_op jit(solution)/shard_map/lscf,slcd->lfd/dot_general | solution.py:77
  101.4 2.3 %fusion.62 = (bf16[8,1,4,36,768]{4,0,3,2,1:T(8,128)(2,1)S(1)}, bf16[8,1,4,36,768]{4,0,3,2,1:T(8,128)(2,1)S(1)}) fusion(bf16[8,2,4,36,768]{4,0,3,2,1:T(8,128)(2,1)} %collective-permute-done.1), kind=kLoop, calls=%fused_computation.102 | loop fusion | bytes 7077888 | tf_op jit(solution)/shard_map/slice | solution.py:31
  103.8 1.6 %fusion.9 = f32[4,8,36]{2,0,1:T(4,128)S(1)} fusion(bf16[4,1,8,36,512]{4,3,2,1,0:T(8,128)(2,1)S(1)} %copy-done.9, bf16[8,768,512]{2,1,0:T(8,128)(2,1)S(1)} %bitcast.151, bf16[8,1,4,36,768]{4,0,3,2,1:T(8,128)(2,1)S(1)} %get-tuple-element.24), kind=kOutput, calls=%fused_computation.19 | convolution fusion | flops 907737984 | bytes 9245184 | tf_op jit(solution)/shard_map/lscf,lfd->slcd/dot_general | solution.py:82
  105.4 1.8 %fusion.10 = f32[4,8,36]{2,0,1:T(4,128)S(1)} fusion(bf16[4,1,8,36,512]{4,3,2,1,0:T(8,128)(2,1)S(1)} %copy-done.8, bf16[8,768,512]{2,1,0:T(8,128)(2,1)S(1)} %bitcast.151, bf16[8,1,4,36,768]{4,0,3,2,1:T(8,128)(2,1)S(1)} %get-tuple-element.25), kind=kOutput, calls=%fused_computation.21 | convolution fusion | flops 907737984 | bytes 9245184 | tf_op jit(solution)/shard_map/lscf,lfd->slcd/dot_general | solution.py:82
  107.1 0.6 copy_dynamic-update-slice_fusion.1
  107.8 0.6 copy_dynamic-update-slice_fusion
  108.4 1.6 %reshape.69 = f32[16,1,288]{2,1,0:T(1,128)} reshape(f32[16,8,36]{2,1,0:T(8,128)} %bitcast.44) | data formatting | bytes 36864
  109.9 4.1 %all-to-all-start.1 = ((f32[16,1,288]{2,1,0:T(1,128)}), f32[16,1,288]{2,1,0:T(1,128)}, u32[]{:S(2)}, u32[]{:S(2)}) async-start(f32[16,1,288]{2,1,0:T(1,128)} %reshape.69), calls=%async_computation.1 | async-start | bytes 49152 | tf_op jit(solution)/shard_map/all_to_all | solution.py:86
  114.1 3.4 %fusion.17 = bf16[8,768,512,1]{1,2,3,0:T(8,128)(2,1)S(1)} fusion(bf16[8,1,4,36,768]{4,0,3,2,1:T(8,128)(2,1)S(1)} %get-tuple-element.25, bf16[4,1,8,36,512]{4,3,2,1,0:T(8,128)(2,1)} %get-tuple-element.35), kind=kOutput, calls=%fused_computation.37 | convolution fusion | flops 905969664 | bytes 9240576 | tf_op jit(solution)/shard_map/lscf,slcd->lfd/dot_general | solution.py:77
  117.4 1.9 %fusion.18 = bf16[8,768,512,1]{1,2,3,0:T(8,128)(2,1)S(1)} fusion(bf16[8,1,4,36,768]{4,0,3,2,1:T(8,128)(2,1)S(1)} %get-tuple-element.24, bf16[4,1,8,36,512]{4,3,2,1,0:T(8,128)(2,1)S(1)} %copy-done), kind=kOutput, calls=%fused_computation.38 | convolution fusion | flops 905969664 | bytes 9240576 | tf_op jit(solution)/shard_map/lscf,slcd->lfd/dot_general | solution.py:77
  119.4 9.5 %fusion = f32[8,768,512]{1,2,0:T(8,128)} fusion(bf16[8,512,768,1]{2,1,3,0:T(8,128)(2,1)} %fusion.22, bf16[8,768,512,1]{1,2,3,0:T(8,128)(2,1)S(1)} %fusion.17, bf16[8,768,512,1]{1,2,3,0:T(8,128)(2,1)S(1)} %fusion.18, bf16[8,1,4,36,768]{4,0,3,2,1:T(8,128)(2,1)S(1)} %copy-done.5, bf16[4,1,8,36,512]{4,3,2,1,0:T(8,128)(2,1)} %get-tuple-element.37), kind=kOutput, calls=%fused_computation.3 | convolution fusion | flops 931135488 | bytes 34406400 | tf_op jit(solution)/shard_map/lscf,slcd->lfd/dot_general | solution.py:77
  128.9 12.6 %copy.190 = f32[8,768,512]{2,1,0:T(8,128)} copy(f32[8,768,512]{1,2,0:T(8,128)} %fusion) | data formatting | bytes 25165824
  141.5 0.5 broadcast.17
  142.0 1.4 reduce
  143.6 0.8 select_reduce_fusion
  144.5 0.6 select_reduce_fusion.1
  (47 shorter events, 0.7 us)
Async XLA Ops:
  7.2 66.9 %all-gather.3.cloned.1.call-start = ((), (), s32[]{:S(2)}) async-start(), calls=%async_computation.2 | async-start | bytes 2785280 | tf_op jit(solution)/shard_map/all_gather | solution.py:41
  10.9 14.0 %copy-start.6 = (bf16[8,1,4,36,768]{4,2,3,1,0:T(4,128)(2,1)S(1)}, bf16[8,1,4,36,768]{4,2,3,1,0:T(4,128)(2,1)}, u32[]{:S(2)}) copy-start(bf16[8,1,4,36,768]{4,2,3,1,0:T(4,128)(2,1)} %param.8) | copy-start | bytes 5308420
  24.8 1.0 copy-start.13
  25.4 40.5 %collective-permute-start = (bf16[8,1,4,36,768]{4,0,3,2,1:T(8,128)(2,1)S(1)}, bf16[8,1,4,36,768]{4,0,3,2,1:T(8,128)(2,1)S(1)}, u32[]{:S(2)}, u32[]{:S(2)}) collective-permute-start(bf16[8,1,4,36,768]{4,0,3,2,1:T(8,128)(2,1)S(1)} %copy.170), channel_id=1, source_target_pairs={{0,2},{1,3},{2,0},{3,1},{4,6},{5,7},{6,4},{7,5},{8,10},{9,11},{10,... | collective-permute-start | bytes 5308424 | tf_op jit(solution)/shard_map/ppermute | solution.py:27
  65.9 2.4 %copy-start.3 = (bf16[8,1,4,36,768]{4,0,3,2,1:T(8,128)(2,1)}, bf16[8,1,4,36,768]{4,0,3,2,1:T(8,128)(2,1)S(1)}, u32[]{:S(2)}) copy-start(bf16[8,1,4,36,768]{4,0,3,2,1:T(8,128)(2,1)S(1)} %collective-permute-done) | copy-start | bytes 5308420
  68.3 33.1 %collective-permute-start.1 = (bf16[8,2,4,36,768]{4,0,3,2,1:T(8,128)(2,1)}, bf16[8,2,4,36,768]{4,0,3,2,1:T(8,128)(2,1)}, u32[]{:S(2)}, u32[]{:S(2)}) collective-permute-start(bf16[8,2,4,36,768]{4,0,3,2,1:T(8,128)(2,1)} %pad_maximum_fusion), channel_id=1, source_target_pairs={{0,1},{1,0},{2,3},{3,2},{4,5},{5,4},{6,7},{7,6},{8,9},{9,8},{10,11... | collective-permute-start | bytes 10616840 | tf_op jit(solution)/shard_map/ppermute | solution.py:28
  75.4 2.9 %copy-start.1 = (bf16[16,132,1,512]{3,1,2,0:T(8,128)(2,1)S(1)}, bf16[16,132,1,512]{3,1,2,0:T(8,128)(2,1)}, u32[]{:S(2)}) copy-start(bf16[16,132,1,512]{3,1,2,0:T(8,128)(2,1)} %all-gather.3.cloned.1.call-done) | copy-start | bytes 6488068
  78.2 1.6 %copy-start.2 = (bf16[16,132,1,512]{3,1,2,0:T(8,128)(2,1)S(1)}, bf16[16,132,1,512]{3,1,2,0:T(8,128)(2,1)}, u32[]{:S(2)}) copy-start(bf16[16,132,1,512]{3,1,2,0:T(8,128)(2,1)} %all-gather.3.cloned.1.call-done) | copy-start | bytes 6488068
  85.5 6.3 %copy-start.4 = (bf16[8,1,4,36,768]{4,0,3,2,1:T(8,128)(2,1)S(1)}, bf16[8,1,4,36,768]{4,0,3,2,1:T(8,128)(2,1)}, u32[]{:S(2)}) copy-start(bf16[8,1,4,36,768]{4,0,3,2,1:T(8,128)(2,1)} %copy-done.3) | copy-start | bytes 5308420
  85.5 6.3 %copy-start.11 = (bf16[4,1,8,36,512]{4,3,2,1,0:T(8,128)(2,1)S(1)}, bf16[4,1,8,36,512]{4,3,2,1,0:T(8,128)(2,1)}, u32[]{:S(2)}) copy-start(bf16[4,1,8,36,512]{4,3,2,1,0:T(8,128)(2,1)} %get-tuple-element.18) | copy-start | bytes 3538948
  91.8 5.0 %copy-start.7 = (bf16[8,1,4,36,768]{4,2,3,1,0:T(4,128)(2,1)S(1)}, bf16[8,1,4,36,768]{4,2,3,1,0:T(4,128)(2,1)}, u32[]{:S(2)}) copy-start(bf16[8,1,4,36,768]{4,2,3,1,0:T(4,128)(2,1)} %param.8) | copy-start | bytes 5308420
  91.8 5.0 %copy-start.10 = (bf16[4,1,8,36,512]{4,3,2,1,0:T(8,128)(2,1)S(1)}, bf16[4,1,8,36,512]{4,3,2,1,0:T(8,128)(2,1)}, u32[]{:S(2)}) copy-start(bf16[4,1,8,36,512]{4,3,2,1,0:T(8,128)(2,1)} %get-tuple-element.34) | copy-start | bytes 3538948
  91.8 12.0 %slice-start = ((s8[6291456]{0:T(1024)(128)(4,1)}), s8[2097152]{0:T(1024)(128)(4,1)S(1)}, s32[]{:S(2)}) async-start(s8[6291456]{0:T(1024)(128)(4,1)} %bitcast.150), calls=%async_computation.3 | async-start | bytes 4194304
  96.8 7.0 %slice-start.1 = ((s8[6291456]{0:T(1024)(128)(4,1)}), s8[4194304]{0:T(1024)(128)(4,1)S(1)}, s32[]{:S(2)}) async-start(s8[6291456]{0:T(1024)(128)(4,1)} %bitcast.150), calls=%async_computation.4 | async-start | bytes 8388608
  101.4 2.4 %copy-start.9 = (bf16[4,1,8,36,512]{4,3,2,1,0:T(8,128)(2,1)S(1)}, bf16[4,1,8,36,512]{4,3,2,1,0:T(8,128)(2,1)}, u32[]{:S(2)}) copy-start(bf16[4,1,8,36,512]{4,3,2,1,0:T(8,128)(2,1)} %get-tuple-element.16) | copy-start | bytes 3538948
  103.8 1.6 %copy-start.8 = (bf16[4,1,8,36,512]{4,3,2,1,0:T(8,128)(2,1)S(1)}, bf16[4,1,8,36,512]{4,3,2,1,0:T(8,128)(2,1)}, u32[]{:S(2)}) copy-start(bf16[4,1,8,36,512]{4,3,2,1,0:T(8,128)(2,1)} %get-tuple-element.17) | copy-start | bytes 3538948
  109.9 31.6 %all-to-all-start.1 = ((f32[16,1,288]{2,1,0:T(1,128)}), f32[16,1,288]{2,1,0:T(1,128)}, u32[]{:S(2)}, u32[]{:S(2)}) async-start(f32[16,1,288]{2,1,0:T(1,128)} %reshape.69), calls=%async_computation.1 | async-start | bytes 49152 | tf_op jit(solution)/shard_map/all_to_all | solution.py:86
  114.0 3.4 %copy-start = (bf16[4,1,8,36,512]{4,3,2,1,0:T(8,128)(2,1)S(1)}, bf16[4,1,8,36,512]{4,3,2,1,0:T(8,128)(2,1)}, u32[]{:S(2)}) copy-start(bf16[4,1,8,36,512]{4,3,2,1,0:T(8,128)(2,1)} %get-tuple-element.36) | copy-start | bytes 3538948
  117.4 2.0 %copy-start.5 = (bf16[8,1,4,36,768]{4,0,3,2,1:T(8,128)(2,1)S(1)}, bf16[8,1,4,36,768]{4,0,3,2,1:T(8,128)(2,1)}, u32[]{:S(2)}) copy-start(bf16[8,1,4,36,768]{4,0,3,2,1:T(8,128)(2,1)} %copy-done.3) | copy-start | bytes 5308420
  128.9 14.8 %copy-start.12 = (pred[128,8,32]{0,2,1:T(8,128)(4,1)S(1)}, pred[128,8,32]{0,2,1:T(8,128)(4,1)}, u32[]{:S(2)}) copy-start(pred[128,8,32]{0,2,1:T(8,128)(4,1)} %get-tuple-element.33) | copy-start | bytes 98308
Sparse Core Ops, SparseCore 0:
  24.9 49.0 all-gather.2
